TPU v7x, 32 devices: a whole 2x2x4 slice. The times are simulated.
32 devices in a mesh: dom: 4 (over y, x), grp: 8 (over z, core).
Axes of the slice: x: 2, y: 2, z: 4, core: 2. Of those that a mesh axis runs over, the one named last changes fastest.
Arguments:
- features: bfloat16 [40960, 128], P(('dom', 'grp')), may hold values from -6 to 6
- send_dom: int32 [32, 4, 32], P(('dom', 'grp')), may hold values from 0 to 1279
- send_grp: int32 [32, 8, 32], P(('dom', 'grp')), may hold values from 0 to 1279
- tile_vals: bfloat16 [1536, 128, 128], P(('dom', 'grp')), may hold values from 0.049804688 to 1
- tile_tgt: int32 [1536], P(('dom', 'grp')), may hold values from 0 to 9, as said below
- tile_src: int32 [1536], P(('dom', 'grp')), may hold values from 0 to 12, as said below
- tile_count: int32 [32], P(('dom', 'grp')), may hold values from 13 to 48, as said below
- w_self: bfloat16 [128, 256], replicated, may hold values from -0.5 to 0.5
- w_neigh: bfloat16 [128, 256], replicated, may hold values from -0.5 to 0.5
- cotangent: bfloat16 [40960, 256], P(('dom', 'grp'))
Outputs:
- output: bfloat16 [40960, 256], P(('dom', 'grp'))
- grad_features: bfloat16 [40960, 128], P(('dom', 'grp'))
- grad_self: float32 [128, 256], replicated
- grad_neigh: float32 [128, 256], replicated
Inputs may be any that keep to these rules, and one draw needn't show every extreme that they name: `tile_tgt`: in every partition, tile slot t for t < 10 has target block t; other slots name any target block. `tile_src`: in every partition, tile slot t for t < 13 has source block t; other slots name any source block. `tile_count`: some partition has all 48 slots live in every draw.
All inputs are finite; a program needn't handle non-finite values.
Results may differ from a plain program's by a relative error of at most 0.0049.
Values may be sent and summed in bfloat16 or wider, within the bound.
No kernel may reach another device: no remote copies, remote signals or barrier semaphores. Data moves between devices by JAX's collectives and lax.ppermute only.
A program may use at most 64 MiB of HBM per device.

v0:
```python
import jax
import jax.numpy as jnp
from jax import lax
from jax.sharding import PartitionSpec as P


def per_device(
    features,
    send_dom,
    send_grp,
    tile_vals,
    tile_tgt,
    tile_src,
    tile_count,
    w_self,
    w_neigh,
    cotangent,
):
    tile_size = tile_vals.shape[1]
    width = features.shape[1]
    node_count = features.shape[0]
    block_count = node_count // tile_size
    dom_index = send_dom[0]
    grp_index = send_grp[0]
    dom_peers = dom_index.shape[0]
    recv_dom = lax.all_to_all(features[dom_index], "dom", split_axis=0, concat_axis=0, tiled=True)
    recv_grp = lax.all_to_all(features[grp_index], "grp", split_axis=0, concat_axis=0, tiled=True)
    source = jnp.concatenate(
        [features, recv_dom.reshape(-1, width), recv_grp.reshape(-1, width)], axis=0
    )
    source = source.reshape(-1, tile_size, width)
    source_count = source.shape[0]
    slot_count = tile_vals.shape[0]
    usable = jnp.arange(slot_count, dtype=jnp.int32) < tile_count[0]
    to_target = (
        (tile_tgt[None, :] == jnp.arange(block_count, dtype=jnp.int32)[:, None]) & usable[None, :]
    ).astype(jnp.float32)
    to_source = (
        (tile_src[None, :] == jnp.arange(source_count, dtype=jnp.int32)[:, None]) & usable[None, :]
    ).astype(jnp.float32)
    products = jnp.einsum(
        "tij,tjf->tif", tile_vals, source[tile_src], preferred_element_type=jnp.float32
    )
    summed = jnp.einsum("bt,tif->bif", to_target, products, precision=lax.Precision.HIGHEST)
    unit_column = jnp.ones((tile_size,), jnp.bfloat16)
    row_sums = jnp.einsum("tij,j->ti", tile_vals, unit_column, preferred_element_type=jnp.float32)
    degree = jnp.dot(to_target, row_sums, precision=lax.Precision.HIGHEST)
    agg = (summed / degree[:, :, None]).reshape(node_count, width).astype(jnp.bfloat16)
    preact = jnp.dot(features, w_self, preferred_element_type=jnp.float32) + jnp.dot(
        agg, w_neigh, preferred_element_type=jnp.float32
    )
    sigm = jax.nn.sigmoid(preact)
    output = (preact * sigm).astype(jnp.bfloat16)
    grad_pre = (cotangent.astype(jnp.float32) * sigm * (1.0 + preact * (1.0 - sigm))).astype(
        jnp.bfloat16
    )
    part_self = jnp.einsum("nf,nh->fh", features, grad_pre, preferred_element_type=jnp.float32)
    part_neigh = jnp.einsum("nf,nh->fh", agg, grad_pre, preferred_element_type=jnp.float32)
    grad_own = jnp.einsum("nh,fh->nf", grad_pre, w_self, preferred_element_type=jnp.float32)
    grad_agg = jnp.einsum("nh,fh->nf", grad_pre, w_neigh, preferred_element_type=jnp.float32)
    grad_agg = (grad_agg / degree.reshape(-1)[:, None]).astype(jnp.bfloat16)
    picked = grad_agg.reshape(block_count, tile_size, width)[tile_tgt]
    backward = jnp.einsum("tij,tif->tjf", tile_vals, picked, preferred_element_type=jnp.float32)
    grad_source = jnp.einsum(
        "st,tjf->sjf", to_source, backward, precision=lax.Precision.HIGHEST
    ).reshape(-1, width)
    dom_rows = dom_peers * dom_index.shape[1]
    back_dom = (
        grad_source[node_count : node_count + dom_rows]
        .reshape(dom_index.shape[0], dom_index.shape[1], width)
        .astype(jnp.bfloat16)
    )
    back_grp = (
        grad_source[node_count + dom_rows :]
        .reshape(grp_index.shape[0], grp_index.shape[1], width)
        .astype(jnp.bfloat16)
    )
    ret_dom = lax.all_to_all(back_dom, "dom", split_axis=0, concat_axis=0, tiled=True)
    ret_grp = lax.all_to_all(back_grp, "grp", split_axis=0, concat_axis=0, tiled=True)
    grad_self, grad_neigh = lax.psum((part_self, part_neigh), ("dom", "grp"))
    grad_total = grad_own + grad_source[:node_count]
    grad_total = grad_total.at[dom_index.reshape(-1)].add(
        ret_dom.reshape(-1, width).astype(jnp.float32)
    )
    grad_total = grad_total.at[grp_index.reshape(-1)].add(
        ret_grp.reshape(-1, width).astype(jnp.float32)
    )
    return (output, grad_total.astype(jnp.bfloat16), grad_self, grad_neigh)


def solution(mesh):
    return jax.shard_map(
        per_device,
        mesh=mesh,
        in_specs=(
            P(("dom", "grp"), None),
            P(("dom", "grp"), None, None),
            P(("dom", "grp"), None, None),
            P(("dom", "grp"), None, None),
            P(("dom", "grp")),
            P(("dom", "grp")),
            P(("dom", "grp")),
            P(),
            P(),
            P(("dom", "grp"), None),
        ),
        out_specs=(P(("dom", "grp"), None), P(("dom", "grp"), None), P(), P()),
        check_vma=False,
    )
```

profile of v0, /device:TPU:0, one launch (start us, length us, event | category | flops | bytes accessed | tf_op | source)
XLA Modules:
  0.0 210.0 jit_solution(4787525386066854471)
XLA Ops:
  7.2 0.8 compare_select_fusion.2
  8.1 2.3 %gather_fusion = bf16[128,128]{1,0:T(8,128)(2,1)} fusion(bf16[1280,128]{1,0:T(8,128)(2,1)} %param.10, s32[1024]{0:T(1024)S(1)} %pad_clamp_fusion.3), kind=kCustom, calls=%fused_computation | custom fusion | bytes 66048 | tf_op jit(solution)/shard_map/gather | solution.py:26
  10.4 5.2 %all-to-all-start = ((bf16[4,32,128]{2,1,0:T(8,128)(2,1)}), bf16[4,32,128]{2,1,0:T(8,128)(2,1)S(1)}, u32[]{:S(2)}, u32[]{:S(2)}) async-start(bf16[4,32,128]{2,1,0:T(8,128)(2,1)} %bitcast.3), calls=%async_computation | async-start | bytes 65536 | tf_op jit(solution)/shard_map/all_to_all | solution.py:26
  15.6 0.8 reshape_squeeze.6
  16.3 0.8 reshape_squeeze.7
  20.4 1.4 fusion.34
  21.9 1.5 gather_fusion.1
  23.4 4.9 %all-to-all-start.1 = ((bf16[8,32,128]{2,1,0:T(8,128)(2,1)}), bf16[8,32,128]{2,1,0:T(8,128)(2,1)S(1)}, u32[]{:S(2)}, u32[]{:S(2)}) async-start(bf16[8,32,128]{2,1,0:T(8,128)(2,1)} %bitcast.6), calls=%async_computation.1 | async-start | bytes 131072 | tf_op jit(solution)/shard_map/all_to_all | solution.py:27
  28.4 5.8 %all-to-all-done.1 = bf16[8,32,128]{2,1,0:T(8,128)(2,1)S(1)} async-done(((bf16[8,32,128]{2,1,0:T(8,128)(2,1)}), bf16[8,32,128]{2,1,0:T(8,128)(2,1)S(1)}, u32[]{:S(2)}, u32[]{:S(2)}) %all-to-all-start.1) | async-done | bytes 65568 | tf_op jit(solution)/shard_map/all_to_all | solution.py:27
  34.2 1.9 gather_fusion.2
  36.1 4.3 %fusion.35 = f32[48,128,128]{2,1,0:T(8,128)} fusion(bf16[48,128,128]{2,1,0:T(8,128)(2,1)} %gather_fusion.2, bf16[48,128,128]{2,1,0:T(8,128)(2,1)S(1)} %copy-done), kind=kOutput, calls=%fused_computation.55 | convolution fusion | flops 201326592 | bytes 6291456 | tf_op jit(solution)/shard_map/tij,tjf->tif/dot_general | solution.py:41
  40.4 3.6 %copy.22 = f32[48,128,128]{1,0,2:T(8,128)} copy(f32[48,128,128]{2,1,0:T(8,128)} %fusion.35) | data formatting | bytes 6291456 | tf_op jit(solution)/shard_map/tij,tjf->tif/dot_general | solution.py:41
  44.1 3.3 %fusion.8 = bf16[10,128,128]{2,0,1:T(8,128)(2,1)S(1)} fusion(f32[48,128,128]{1,0,2:T(8,128)} %copy.22, f32[10,128]{0,1:T(8,128)S(1)} %copy.17, s32[48]{0:T(128)S(1)} %copy-done.5, pred[48]{0:T(512)(128)(4,1)S(1)} %iota_compare_fusion.2), kind=kOutput, calls=%fused_computation.18 | convolution fusion | flops 94700480 | bytes 3478768 | tf_op jit(solution)/shard_map/bt,tif->bif/dot_general | solution.py:44
  47.5 1.6 multiply_convert_fusion
  49.1 1.0 fusion.37
  50.4 1.9 gather_fusion.3
  52.3 3.7 %fusion.36 = f32[48,128,128]{2,1,0:T(8,128)} fusion(bf16[48,128,128]{2,1,0:T(8,128)(2,1)} %gather_fusion.3, bf16[48,128,128]{2,1,0:T(8,128)(2,1)S(1)} %copy-done), kind=kOutput, calls=%fused_computation.56 | convolution fusion | flops 201326592 | bytes 6291456 | tf_op jit(solution)/shard_map/tij,tif->tjf/dot_general | solution.py:63
  56.1 3.6 %copy.24 = f32[48,128,128]{1,0,2:T(8,128)} copy(f32[48,128,128]{2,1,0:T(8,128)} %fusion.36) | data formatting | bytes 6291456 | tf_op jit(solution)/shard_map/tij,tif->tjf/dot_general | solution.py:63
  59.7 4.0 %fusion.33 = (bf16[13,128,128]{2,0,1:T(8,128)(2,1)S(1)}, f32[13,128,128]{2,0,1:T(8,128)}) fusion(f32[48,128,128]{1,0,2:T(8,128)} %copy.24, s32[48]{0:T(128)S(1)} %copy-done.6, pred[48]{0:T(512)(128)(4,1)S(1)} %iota_compare_fusion.2), kind=kOutput, calls=%fused_computation.53 | convolution fusion | flops 122897632 | bytes 4423920 | tf_op jit(solution)/shard_map/st,tjf->sjf/dot_general | solution.py:64
  64.4 4.2 %all-to-all-start.2 = ((bf16[4,32,128]{2,1,0:T(8,128)(2,1)}), bf16[4,32,128]{2,1,0:T(8,128)(2,1)S(1)}, u32[]{:S(2)}, u32[]{:S(2)}) async-start(bf16[4,32,128]{2,1,0:T(8,128)(2,1)} %bitcast.26), calls=%async_computation.2 | async-start | bytes 65536 | tf_op jit(solution)/shard_map/all_to_all | solution.py:78
  68.6 1.0 convolution_bitcast_fusion
  69.7 1.4 copy.19
  71.8 1.5 all-to-all-done.2
  73.4 3.4 %all-to-all-start.3 = ((bf16[8,32,128]{2,1,0:T(8,128)(2,1)}), bf16[8,32,128]{2,1,0:T(8,128)(2,1)S(1)}, u32[]{:S(2)}, u32[]{:S(2)}) async-start(bf16[8,32,128]{2,1,0:T(8,128)(2,1)} %bitcast.21), calls=%async_computation.3 | async-start | bytes 131072 | tf_op jit(solution)/shard_map/all_to_all | solution.py:79
  76.8 1.2 convolution_add_fusion.1
  77.9 3.1 %scatter_custom_fusion = f32[1280,128]{1,0:T(8,128)} fusion(f32[1280,128]{1,0:T(8,128)} %convolution_add_fusion.1, s32[128]{0:T(128)S(1)} %fusion.29, bf16[128,128]{1,0:T(8,128)(2,1)S(1)} %bitcast.80), kind=kCustom, calls=%fused_computation.23 | custom fusion | flops 32768 | bytes 688128 | tf_op jit(solution)/shard_map/scatter-add | solution.py:82
  81.0 1.6 all-to-all-done.3
  82.6 3.7 %scatter_custom_fusion.1 = f32[1280,128]{1,0:T(8,128)} fusion(f32[1280,128]{1,0:T(8,128)} %scatter_custom_fusion, s32[256]{0:T(256)S(1)} %bitcast.83, bf16[256,128]{1,0:T(8,128)(2,1)S(1)} %bitcast.77), kind=kCustom, calls=%fused_computation.21 | custom fusion | flops 65536 | bytes 720896 | tf_op jit(solution)/shard_map/scatter-add | solution.py:85
  86.3 1.8 convert_element_type.55
  88.1 111.7 %all-reduce.3.cloned.1.call-done = (f32[128,256]{0,1:T(8,128)}, f32[128,256]{1,0:T(8,128)}) async-done(((f32[128,256]{0,1:T(8,128)}, f32[128,256]{1,0:T(8,128)}), (f32[128,256]{0,1:T(8,128)}, f32[128,256]{1,0:T(8,128)})) %all-reduce.3.cloned.1.call-update) | async-done | bytes 262160 | tf_op jit(solution)/shard_map/psum | solution.py:80
  199.9 1.7 copy.21
  201.5 1.6 copy.31
  (43 shorter events, 4.9 us)
Async XLA Ops:
  7.2 12.7 %copy-start = (bf16[48,128,128]{2,1,0:T(8,128)(2,1)S(1)}, bf16[48,128,128]{2,1,0:T(8,128)(2,1)}, u32[]{:S(2)}) copy-start(bf16[48,128,128]{2,1,0:T(8,128)(2,1)} %param.13) | copy-start | bytes 4718596
  7.2 13.2 %copy-start.1 = (bf16[1280,128]{1,0:T(8,128)(2,1)S(1)}, bf16[1280,128]{1,0:T(8,128)(2,1)}, u32[]{:S(2)}) copy-start(bf16[1280,128]{1,0:T(8,128)(2,1)} %param.10) | copy-start | bytes 983044
  7.2 13.2 %copy-start.3 = (bf16[128,256]{1,0:T(8,128)(2,1)S(1)}, bf16[128,256]{1,0:T(8,128)(2,1)}, u32[]{:S(2)}) copy-start(bf16[128,256]{1,0:T(8,128)(2,1)} %param.17) | copy-start | bytes 196612
  10.4 13.0 %all-to-all-start = ((bf16[4,32,128]{2,1,0:T(8,128)(2,1)}), bf16[4,32,128]{2,1,0:T(8,128)(2,1)S(1)}, u32[]{:S(2)}, u32[]{:S(2)}) async-start(bf16[4,32,128]{2,1,0:T(8,128)(2,1)} %bitcast.3), calls=%async_computation | async-start | bytes 65536 | tf_op jit(solution)/shard_map/all_to_all | solution.py:26
  19.8 1.9 copy-start.5
  23.4 10.8 %all-to-all-start.1 = ((bf16[8,32,128]{2,1,0:T(8,128)(2,1)}), bf16[8,32,128]{2,1,0:T(8,128)(2,1)S(1)}, u32[]{:S(2)}, u32[]{:S(2)}) async-start(bf16[8,32,128]{2,1,0:T(8,128)(2,1)} %bitcast.6), calls=%async_computation.1 | async-start | bytes 131072 | tf_op jit(solution)/shard_map/all_to_all | solution.py:27
  44.1 3.4 %copy-start.2 = (f32[1280,256]{1,0:T(8,128)S(1)}, f32[1280,256]{1,0:T(8,128)}, u32[]{:S(2)}) copy-start(f32[1280,256]{1,0:T(8,128)} %fusion.34) | copy-start | bytes 3932164
  44.1 3.4 %copy-start.7 = (bf16[1280,256]{1,0:T(8,128)(2,1)S(1)}, bf16[1280,256]{1,0:T(8,128)(2,1)}, u32[]{:S(2)}) copy-start(bf16[1280,256]{1,0:T(8,128)(2,1)} %param.19) | copy-start | bytes 1966084
  44.1 3.4 %copy-start.8 = (bf16[128,256]{1,0:T(8,128)(2,1)S(1)}, bf16[128,256]{1,0:T(8,128)(2,1)}, u32[]{:S(2)}) copy-start(bf16[128,256]{1,0:T(8,128)(2,1)} %param.18) | copy-start | bytes 196612
  56.1 3.6 %copy-start.6 = (s32[48]{0:T(128)S(1)}, s32[48]{0:T(128)}, u32[]{:S(2)}) copy-start(s32[48]{0:T(128)} %param.15) | copy-start | bytes 580
  64.4 9.0 %all-to-all-start.2 = ((bf16[4,32,128]{2,1,0:T(8,128)(2,1)}), bf16[4,32,128]{2,1,0:T(8,128)(2,1)S(1)}, u32[]{:S(2)}, u32[]{:S(2)}) async-start(bf16[4,32,128]{2,1,0:T(8,128)(2,1)} %bitcast.26), calls=%async_computation.2 | async-start | bytes 65536 | tf_op jit(solution)/shard_map/all_to_all | solution.py:78
  68.6 8.1 %copy-start.4 = (bf16[128,256]{1,0:T(8,128)(2,1)S(1)}, bf16[128,256]{1,0:T(8,128)(2,1)}, u32[]{:S(2)}) copy-start(bf16[128,256]{1,0:T(8,128)(2,1)} %param.17) | copy-start | bytes 196612
  68.6 131.3 %all-reduce.3.cloned.1.call-start = ((), (), s32[]{:S(2)}) async-start(), calls=%async_computation.4 | async-start | bytes 524288 | tf_op jit(solution)/shard_map/psum | solution.py:80
  73.4 9.2 %all-to-all-start.3 = ((bf16[8,32,128]{2,1,0:T(8,128)(2,1)}), bf16[8,32,128]{2,1,0:T(8,128)(2,1)S(1)}, u32[]{:S(2)}, u32[]{:S(2)}) async-start(bf16[8,32,128]{2,1,0:T(8,128)(2,1)} %bitcast.21), calls=%async_computation.3 | async-start | bytes 131072 | tf_op jit(solution)/shard_map/all_to_all | solution.py:79
Sparse Core Ops, SparseCore 0:
  75.7 124.1 all-reduce.2
where the time goes:
time: 211 us; the launch traced here: 210 us
  waiting for transfers between devices  121 us (57%)
  local copies, waits for them, and re-layouts  22.9 us (11%)
  matrix products  22.5 us (11%)
  starting transfers between devices  17.6 us (8%)
  between operations  14.8 us (7%)
  other arithmetic  11.5 us (5%)
    psum x1, waiting for transfers between devices, per_device(): grad_self, grad_neigh = lax.psum((part_self, part_neigh), ('dom', 'grp'))  112 us
    all_to_all x1, waiting for transfers between devices, per_device(): lax.all_to_all(features[grp_index], 'grp', split_axis=0, concat_axis=0, t...  5.79 us
    all_to_all x1, starting transfers between devices, per_device(): lax.all_to_all(features[dom_index], 'dom', split_axis=0, concat_axis=0, t...  5.16 us
    all_to_all x1, starting transfers between devices, per_device(): lax.all_to_all(features[grp_index], 'grp', split_axis=0, concat_axis=0, t...  4.88 us
    dot_general x1, matrix products, per_device(): jnp.einsum('tij,tjf->tif', tile_vals, source[tile_src], preferred_element...  4.3 us
  transfers between devices with their start and end apart: 5, of which 4 were waited for; matrix products, arithmetic and copies ran while one was open for 10% of the time, Pallas kernels for 0%

commit v1 on v0

--- a/solution.py
+++ b/solution.py
@@ -77,7 +77,7 @@
     )
     ret_dom = lax.all_to_all(back_dom, "dom", split_axis=0, concat_axis=0, tiled=True)
     ret_grp = lax.all_to_all(back_grp, "grp", split_axis=0, concat_axis=0, tiled=True)
-    grad_self, grad_neigh = lax.psum((part_self, part_neigh), ("dom", "grp"))
+    grad_self, grad_neigh = lax.psum(lax.psum((part_self, part_neigh), "grp"), "dom")
     grad_total = grad_own + grad_source[:node_count]
     grad_total = grad_total.at[dom_index.reshape(-1)].add(
         ret_dom.reshape(-1, width).astype(jnp.float32)

time: 211 us -> 180 us (0.85)
  waiting for transfers between devices: 121 us -> 96.7 us
  other arithmetic: 11.5 us -> 7.36 us
  matrix products: 22.5 us -> 20.3 us
    psum x1 -> x2, waiting for transfers between devices: 112 us -> 87.4 us  [the longest x1 54.4 us: per_device(): lax.psum((part_self, part_neigh), 'grp')]
    unnamed x21 -> x27, local copies, waits for them, and re-layouts: 3.88 us -> 4.67 us
  transfers between devices with their start and end apart: 5 -> 6, of which waited for: 4 -> 4; matrix products, arithmetic and copies ran while one was open for 10% -> 8% of each run, Pallas kernels for 0% -> 0%
where the time goes in v1:
time: 180 us; the launch traced here: 179 us
  waiting for transfers between devices  96.7 us (54%)
  local copies, waits for them, and re-layouts  22.4 us (12%)
  matrix products  20.3 us (11%)
  starting transfers between devices  17.6 us (10%)
  between operations  14.9 us (8%)
  other arithmetic  7.36 us (4%)
    psum x1, waiting for transfers between devices, per_device(): lax.psum((part_self, part_neigh), 'grp')  54.4 us
    psum x1, waiting for transfers between devices, per_device(): lax.psum(lax.psum((part_self, part_neigh), 'grp'), 'dom')  33 us
    all_to_all x1, waiting for transfers between devices, per_device(): lax.all_to_all(features[grp_index], 'grp', split_axis=0, concat_axis=0, t...  5.7 us
    all_to_all x1, starting transfers between devices, per_device(): lax.all_to_all(features[dom_index], 'dom', split_axis=0, concat_axis=0, t...  5.16 us
    all_to_all x1, starting transfers between devices, per_device(): lax.all_to_all(features[grp_index], 'grp', split_axis=0, concat_axis=0, t...  4.88 us
    unnamed x27, local copies, waits for them, and re-layouts  4.67 us
    dot_general x1, matrix products, per_device(): jnp.einsum('tij,tjf->tif', tile_vals, source[tile_src], preferred_element...  4.31 us
    all_to_all x1, starting transfers between devices, per_device(): lax.all_to_all(back_dom, 'dom', split_axis=0, concat_axis=0, tiled=True)  4.19 us
  transfers between devices with their start and end apart: 6, of which 4 were waited for; matrix products, arithmetic and copies ran while one was open for 8% of the time, Pallas kernels for 0%

profile of v1, /device:TPU:0, one launch (start us, length us, event | category | flops | bytes accessed | tf_op | source)
XLA Modules:
  0.0 179.4 jit_solution(8764340925082521782)
XLA Ops:
  7.2 0.8 compare_select_fusion.2
  8.1 2.3 %gather_fusion = bf16[128,128]{1,0:T(8,128)(2,1)} fusion(bf16[1280,128]{1,0:T(8,128)(2,1)} %param.10, s32[1024]{0:T(1024)S(1)} %pad_clamp_fusion.3), kind=kCustom, calls=%fused_computation | custom fusion | bytes 66048 | tf_op jit(solution)/shard_map/gather | solution.py:26
  10.4 5.2 %all-to-all-start = ((bf16[4,32,128]{2,1,0:T(8,128)(2,1)}), bf16[4,32,128]{2,1,0:T(8,128)(2,1)S(1)}, u32[]{:S(2)}, u32[]{:S(2)}) async-start(bf16[4,32,128]{2,1,0:T(8,128)(2,1)} %bitcast.3), calls=%async_computation | async-start | bytes 65536 | tf_op jit(solution)/shard_map/all_to_all | solution.py:26
  15.6 0.8 reshape_squeeze.7
  19.6 1.4 fusion.34
  21.1 1.5 gather_fusion.1
  22.6 4.9 %all-to-all-start.1 = ((bf16[8,32,128]{2,1,0:T(8,128)(2,1)}), bf16[8,32,128]{2,1,0:T(8,128)(2,1)S(1)}, u32[]{:S(2)}, u32[]{:S(2)}) async-start(bf16[8,32,128]{2,1,0:T(8,128)(2,1)} %bitcast.6), calls=%async_computation.1 | async-start | bytes 131072 | tf_op jit(solution)/shard_map/all_to_all | solution.py:27
  27.7 5.7 %all-to-all-done.1 = bf16[8,32,128]{2,1,0:T(8,128)(2,1)S(1)} async-done(((bf16[8,32,128]{2,1,0:T(8,128)(2,1)}), bf16[8,32,128]{2,1,0:T(8,128)(2,1)S(1)}, u32[]{:S(2)}, u32[]{:S(2)}) %all-to-all-start.1) | async-done | bytes 65568 | tf_op jit(solution)/shard_map/all_to_all | solution.py:27
  33.4 2.0 %gather_fusion.2 = bf16[48,128,128]{2,1,0:T(8,128)(2,1)} fusion(bf16[13,128,128]{2,1,0:T(8,128)(2,1)S(1)} %bitcast.71, s32[1024]{0:T(1024)S(1)} %pad_clamp_fusion.1), kind=kCustom, calls=%fused_computation.2 | custom fusion | bytes 3145920 | tf_op jit(solution)/shard_map/gather | solution.py:42
  35.4 4.3 %fusion.35 = f32[48,128,128]{2,1,0:T(8,128)} fusion(bf16[48,128,128]{2,1,0:T(8,128)(2,1)} %gather_fusion.2, bf16[48,128,128]{2,1,0:T(8,128)(2,1)S(1)} %copy-done), kind=kOutput, calls=%fused_computation.55 | convolution fusion | flops 201326592 | bytes 6291456 | tf_op jit(solution)/shard_map/tij,tjf->tif/dot_general | solution.py:41
  39.7 3.6 %copy.22 = f32[48,128,128]{1,0,2:T(8,128)} copy(f32[48,128,128]{2,1,0:T(8,128)} %fusion.35) | data formatting | bytes 6291456 | tf_op jit(solution)/shard_map/tij,tjf->tif/dot_general | solution.py:41
  43.3 3.3 %fusion.8 = bf16[10,128,128]{2,0,1:T(8,128)(2,1)S(1)} fusion(f32[48,128,128]{1,0,2:T(8,128)} %copy.22, f32[10,128]{0,1:T(8,128)S(1)} %copy.17, s32[48]{0:T(128)S(1)} %copy-done.8, pred[48]{0:T(512)(128)(4,1)S(1)} %iota_compare_fusion.2), kind=kOutput, calls=%fused_computation.18 | convolution fusion | flops 94700480 | bytes 3478768 | tf_op jit(solution)/shard_map/bt,tif->bif/dot_general | solution.py:44
  46.7 1.7 multiply_convert_fusion
  48.3 1.0 fusion.37
  49.3 1.0 convolution_bitcast_fusion
  50.7 0.8 gather_fusion.3
  51.5 2.3 %fusion.36 = f32[48,128,128]{2,1,0:T(8,128)} fusion(bf16[48,128,128]{2,1,0:T(8,128)(2,1)S(1)} %gather_fusion.3, bf16[48,128,128]{2,1,0:T(8,128)(2,1)S(1)} %copy-done), kind=kOutput, calls=%fused_computation.56 | convolution fusion | flops 201326592 | bytes 6291456 | tf_op jit(solution)/shard_map/tij,tif->tjf/dot_general | solution.py:63
  53.9 3.6 %copy.24 = f32[48,128,128]{1,0,2:T(8,128)} copy(f32[48,128,128]{2,1,0:T(8,128)} %fusion.36) | data formatting | bytes 6291456 | tf_op jit(solution)/shard_map/tij,tif->tjf/dot_general | solution.py:63
  57.5 3.0 %fusion.33 = (bf16[13,128,128]{2,0,1:T(8,128)(2,1)S(1)}, f32[13,128,128]{2,0,1:T(8,128)S(1)}) fusion(f32[48,128,128]{1,0,2:T(8,128)} %copy.24, s32[48]{0:T(128)S(1)} %copy-done.9, pred[48]{0:T(512)(128)(4,1)S(1)} %iota_compare_fusion.2), kind=kOutput, calls=%fused_computation.53 | convolution fusion | flops 122897632 | bytes 4423920 | tf_op jit(solution)/shard_map/st,tjf->sjf/dot_general | solution.py:64
  60.6 0.8 copy-done.5
  62.1 4.2 %all-to-all-start.2 = ((bf16[4,32,128]{2,1,0:T(8,128)(2,1)}), bf16[4,32,128]{2,1,0:T(8,128)(2,1)S(1)}, u32[]{:S(2)}, u32[]{:S(2)}) async-start(bf16[4,32,128]{2,1,0:T(8,128)(2,1)} %bitcast.26), calls=%async_computation.2 | async-start | bytes 65536 | tf_op jit(solution)/shard_map/all_to_all | solution.py:78
  67.0 1.0 slice.30
  68.0 1.0 copy.19
  69.7 54.4 %all-reduce.5.cloned.1.call-done = (f32[128,256]{0,1:T(8,128)}, f32[128,256]{1,0:T(8,128)}) async-done(((f32[128,256]{0,1:T(8,128)}, f32[128,256]{1,0:T(8,128)}), (f32[128,256]{0,1:T(8,128)}, f32[128,256]{1,0:T(8,128)})) %all-reduce.5.cloned.1.call-update) | async-done | bytes 262160 | tf_op jit(solution)/shard_map/psum | solution.py:80
  124.1 3.4 %all-to-all-start.3 = ((bf16[8,32,128]{2,1,0:T(8,128)(2,1)}), bf16[8,32,128]{2,1,0:T(8,128)(2,1)S(1)}, u32[]{:S(2)}, u32[]{:S(2)}) async-start(bf16[8,32,128]{2,1,0:T(8,128)(2,1)} %bitcast.21), calls=%async_computation.3 | async-start | bytes 131072 | tf_op jit(solution)/shard_map/all_to_all | solution.py:79
  127.5 1.4 convolution_add_fusion.1
  128.9 1.5 scatter_custom_fusion
  130.5 2.9 %all-to-all-done.3 = bf16[8,32,128]{2,1,0:T(8,128)(2,1)S(1)} async-done(((bf16[8,32,128]{2,1,0:T(8,128)(2,1)}), bf16[8,32,128]{2,1,0:T(8,128)(2,1)S(1)}, u32[]{:S(2)}, u32[]{:S(2)}) %all-to-all-start.3) | async-done | bytes 65568 | tf_op jit(solution)/shard_map/all_to_all | solution.py:79
  133.4 2.2 %scatter_custom_fusion.1 = f32[1280,128]{1,0:T(8,128)S(1)} fusion(f32[1280,128]{1,0:T(8,128)S(1)} %scatter_custom_fusion, s32[256]{0:T(256)S(1)} %bitcast.83, bf16[256,128]{1,0:T(8,128)(2,1)S(1)} %bitcast.77), kind=kCustom, calls=%fused_computation.21 | custom fusion | flops 65536 | bytes 720896 | tf_op jit(solution)/shard_map/scatter-add | solution.py:85
  136.3 33.0 %all-reduce.7.cloned.1.call-done = (f32[128,256]{0,1:T(8,128)}, f32[128,256]{1,0:T(8,128)}) async-done(((f32[128,256]{0,1:T(8,128)}, f32[128,256]{1,0:T(8,128)}), (f32[128,256]{0,1:T(8,128)}, f32[128,256]{1,0:T(8,128)})) %all-reduce.7.cloned.1.call-update) | async-done | bytes 262160 | tf_op jit(solution)/shard_map/psum | solution.py:80
  169.4 1.7 copy.21
  171.0 1.6 copy.33
  (52 shorter events, 6.4 us)
Async XLA Ops:
  7.2 11.9 %copy-start = (bf16[48,128,128]{2,1,0:T(8,128)(2,1)S(1)}, bf16[48,128,128]{2,1,0:T(8,128)(2,1)}, u32[]{:S(2)}) copy-start(bf16[48,128,128]{2,1,0:T(8,128)(2,1)} %param.13) | copy-start | bytes 4718596
  7.2 12.4 %copy-start.1 = (bf16[1280,128]{1,0:T(8,128)(2,1)S(1)}, bf16[1280,128]{1,0:T(8,128)(2,1)}, u32[]{:S(2)}) copy-start(bf16[1280,128]{1,0:T(8,128)(2,1)} %param.10) | copy-start | bytes 983044
  7.2 12.4 %copy-start.6 = (bf16[128,256]{1,0:T(8,128)(2,1)S(1)}, bf16[128,256]{1,0:T(8,128)(2,1)}, u32[]{:S(2)}) copy-start(bf16[128,256]{1,0:T(8,128)(2,1)} %param.17) | copy-start | bytes 196612
  10.4 12.2 %all-to-all-start = ((bf16[4,32,128]{2,1,0:T(8,128)(2,1)}), bf16[4,32,128]{2,1,0:T(8,128)(2,1)S(1)}, u32[]{:S(2)}, u32[]{:S(2)}) async-start(bf16[4,32,128]{2,1,0:T(8,128)(2,1)} %bitcast.3), calls=%async_computation | async-start | bytes 65536 | tf_op jit(solution)/shard_map/all_to_all | solution.py:26
  19.1 1.9 %copy-start.8 = (s32[48]{0:T(128)S(1)}, s32[48]{0:T(128)}, u32[]{:S(2)}) copy-start(s32[48]{0:T(128)} %param.14) | copy-start | bytes 580
  19.6 7.9 %copy-start.7 = (s32[1,4,32]{2,1,0:T(4,128)S(1)}, s32[1,4,32]{2,1,0:T(4,128)}, u32[]{:S(2)}) copy-start(s32[1,4,32]{2,1,0:T(4,128)} %param.11) | copy-start | bytes 1540
  22.6 10.8 %all-to-all-start.1 = ((bf16[8,32,128]{2,1,0:T(8,128)(2,1)}), bf16[8,32,128]{2,1,0:T(8,128)(2,1)S(1)}, u32[]{:S(2)}, u32[]{:S(2)}) async-start(bf16[8,32,128]{2,1,0:T(8,128)(2,1)} %bitcast.6), calls=%async_computation.1 | async-start | bytes 131072 | tf_op jit(solution)/shard_map/all_to_all | solution.py:27
  43.3 3.4 %copy-start.4 = (f32[1280,256]{1,0:T(8,128)S(1)}, f32[1280,256]{1,0:T(8,128)}, u32[]{:S(2)}) copy-start(f32[1280,256]{1,0:T(8,128)} %fusion.34) | copy-start | bytes 3932164
  43.3 3.4 %copy-start.10 = (bf16[1280,256]{1,0:T(8,128)(2,1)S(1)}, bf16[1280,256]{1,0:T(8,128)(2,1)}, u32[]{:S(2)}) copy-start(bf16[1280,256]{1,0:T(8,128)(2,1)} %param.19) | copy-start | bytes 1966084
  43.3 3.4 %copy-start.11 = (bf16[128,256]{1,0:T(8,128)(2,1)S(1)}, bf16[128,256]{1,0:T(8,128)(2,1)}, u32[]{:S(2)}) copy-start(bf16[128,256]{1,0:T(8,128)(2,1)} %param.18) | copy-start | bytes 196612
  48.3 2.3 %copy-start.2 = (bf16[1280,256]{1,0:T(8,128)(2,1)}, bf16[1280,256]{1,0:T(8,128)(2,1)S(1)}, u32[]{:S(2)}) copy-start(bf16[1280,256]{1,0:T(8,128)(2,1)S(1)} %get-tuple-element.16) | copy-start | bytes 1966084
  53.9 3.6 %copy-start.9 = (s32[48]{0:T(128)S(1)}, s32[48]{0:T(128)}, u32[]{:S(2)}) copy-start(s32[48]{0:T(128)} %param.15) | copy-start | bytes 580
  60.6 0.8 copy-start.5
  60.6 66.9 %copy-start.3 = (bf16[1280,256]{1,0:T(8,128)(2,1)S(1)}, bf16[1280,256]{1,0:T(8,128)(2,1)}, u32[]{:S(2)}) copy-start(bf16[1280,256]{1,0:T(8,128)(2,1)} %copy-done.2) | copy-start | bytes 1966084
  62.1 62.1 %all-to-all-start.2 = ((bf16[4,32,128]{2,1,0:T(8,128)(2,1)}), bf16[4,32,128]{2,1,0:T(8,128)(2,1)S(1)}, u32[]{:S(2)}, u32[]{:S(2)}) async-start(bf16[4,32,128]{2,1,0:T(8,128)(2,1)} %bitcast.26), calls=%async_computation.2 | async-start | bytes 65536 | tf_op jit(solution)/shard_map/all_to_all | solution.py:78
  66.2 57.9 %all-reduce.5.cloned.1.call-start = ((), (), s32[]{:S(2)}) async-start(), calls=%async_computation.4 | async-start | bytes 524288 | tf_op jit(solution)/shard_map/psum | solution.py:80
  67.0 102.4 %all-reduce.7.cloned.1.call-start = ((), (), s32[]{:S(2)}) async-start(), calls=%async_computation.5 | async-start | bytes 524288 | tf_op jit(solution)/shard_map/psum | solution.py:80
  124.1 9.2 %all-to-all-start.3 = ((bf16[8,32,128]{2,1,0:T(8,128)(2,1)}), bf16[8,32,128]{2,1,0:T(8,128)(2,1)S(1)}, u32[]{:S(2)}, u32[]{:S(2)}) async-start(bf16[8,32,128]{2,1,0:T(8,128)(2,1)} %bitcast.21), calls=%async_computation.3 | async-start | bytes 131072 | tf_op jit(solution)/shard_map/all_to_all | solution.py:79
Sparse Core Ops, SparseCore 0:
  70.0 54.0 all-reduce.4
  127.3 42.0 all-reduce.6
